TPU v7x, 512 devices: a whole 4x8x8 slice. The times are simulated.
512 devices in a mesh: section: 8 (over z), ctx: 8 (over y_hi, x), tp: 8 (over y_lo, core).
Axes of the slice: x: 4, y: 8 (y_hi: 2, y_lo: 4; y = y_hi * 4 + y_lo), z: 8, core: 2. Of those that a mesh axis runs over, the one named last changes fastest.
Arguments:
- block_order: int32 [16], replicated, may hold values from 0 to 15, each once
- plan: int32 [8], replicated, may hold values from 0 to 1
- q_box: bfloat16 [8, 2, 1408, 8192], P('section', None, 'ctx', 'tp'), may hold values from -8 to 8
- k_box: bfloat16 [8, 2, 1408, 1024], P('section', None, ('ctx', 'tp')), may hold values from -8 to 8
- v_box: bfloat16 [8, 2, 1408, 1024], P('section', None, ('ctx', 'tp')), may hold values from -6 to 6
- grad_out: bfloat16 [8, 1408, 8192], P('section', 'ctx', 'tp'), may hold values from -6 to 6
Outputs:
- attn_out: bfloat16 [8, 1408, 8192], P('section', 'ctx', 'tp')
- grad_q: bfloat16 [8, 1408, 8192], P('section', 'ctx', 'tp')
- grad_k: float32 [8, 1408, 1024], P('section', ('ctx', 'tp'))
- grad_v: float32 [8, 1408, 1024], P('section', ('ctx', 'tp'))
Inputs may be any that keep to these rules, and one draw needn't show every extreme that they name: `block_order`: a permutation: every block sits in exactly one storage slot, slot j covering storage rows j * 88 to (j + 1) * 88 - 1.
All inputs are finite; a program needn't handle non-finite values.
Results may differ from a plain program's by a relative error of at most 0.012.
Values may be sent and summed in bfloat16 or wider, within the bound.
No kernel may reach another device: no remote copies, remote signals or barrier semaphores. Data moves between devices by JAX's collectives and lax.ppermute only.
A program may use at most 64 MiB of HBM per device.

v0:
```python
import jax
import jax.numpy as jnp
from jax import lax
from jax.sharding import PartitionSpec as P

HEAD_DIM = 128
NEG = -1e30


def passed_along(block, axis, distance):
    devices = range(lax.axis_size(axis))
    route = [((i - distance) % len(devices), i) for i in devices]
    return lax.ppermute(block, axis, route)


def body(block_order, plan, q_box, k_box, v_box, grad_out):
    tp_count = lax.axis_size("tp")
    ctx_count = lax.axis_size("ctx")
    section_count = lax.axis_size("section")
    tok_rows = q_box.shape[2]
    kv_rows = k_box.shape[2]
    seq_rows = tok_rows * ctx_count
    block_len = seq_rows // block_order.shape[0]
    head_size = HEAD_DIM
    heads_local = q_box.shape[3] // head_size
    kv_local = k_box.shape[3] // head_size // tp_count
    group = heads_local // kv_local
    kv_width = kv_local * head_size
    scale = head_size ** (-0.5)
    section_rank = lax.axis_index("section")
    receiver = (section_rank + 1) % section_count
    wanted = lax.dynamic_index_in_dim(plan, receiver, 0, keepdims=False)

    def pick(box):
        slots = box[0]
        chosen = slots[0]
        for slot in range(1, slots.shape[0]):
            chosen = jnp.where(wanted == slot, slots[slot], chosen)
        return chosen

    q_send = pick(q_box)
    k_send = pick(k_box)
    v_send = pick(v_box)
    kv_send = jnp.stack(
        [k_send.reshape(kv_rows, -1, head_size), v_send.reshape(kv_rows, -1, head_size)], axis=2
    ).reshape(kv_rows, -1)
    queries, kv_rows_in = passed_along((q_send, kv_send), "section", 1)
    cotangent = passed_along(grad_out[0], "section", -1)
    plane = ("ctx", "tp")
    kv_pieces = kv_rows_in.reshape(1, kv_rows, tp_count, 2 * kv_width).transpose(0, 2, 1, 3)
    kv_pieces = jnp.broadcast_to(kv_pieces, (ctx_count, tp_count, kv_rows, 2 * kv_width))
    kv_pieces = kv_pieces.reshape(ctx_count * tp_count * kv_rows, 2 * kv_width)
    kv_full = lax.all_to_all(kv_pieces, plane, split_axis=0, concat_axis=0, tiled=True)
    kv_full = kv_full.reshape(seq_rows, kv_local, 2, head_size)
    key_heads = kv_full[:, :, 0, :]
    value_heads = kv_full[:, :, 1, :]
    ctx_rank = lax.axis_index("ctx")
    positions = (
        block_order[:, None] * block_len + jnp.arange(block_len, dtype=jnp.int32)[None, :]
    ).reshape(ctx_count, tok_rows)
    key_pos = positions.reshape(seq_rows)
    query_pos = lax.dynamic_index_in_dim(positions, ctx_rank, 0, keepdims=False)
    visible = (key_pos[None, :] <= query_pos[:, None])[None, None]
    q4 = queries.reshape(tok_rows, kv_local, group, head_size)
    do4 = cotangent.reshape(tok_rows, kv_local, group, head_size)
    scores = jnp.einsum("qgjd,kgd->gjqk", q4, key_heads, preferred_element_type=jnp.float32) * scale
    scores = jnp.where(visible, scores, NEG)
    top_score = jnp.max(scores, axis=-1, keepdims=True)
    totals = jnp.sum(jnp.exp(scores - top_score), axis=-1, keepdims=True)
    log_total = top_score + jnp.log(totals)
    probs = jnp.exp(scores - log_total)
    probs_low = probs.astype(jnp.bfloat16)
    attended = jnp.einsum(
        "gjqk,kgd->qgjd", probs_low, value_heads, preferred_element_type=jnp.float32
    )
    delta = jnp.sum(do4.astype(jnp.float32) * attended, axis=-1)
    dprobs = jnp.einsum("qgjd,kgd->gjqk", do4, value_heads, preferred_element_type=jnp.float32)
    dscores = (probs * (dprobs - jnp.transpose(delta, (1, 2, 0))[..., None])).astype(jnp.bfloat16)
    q_grad = (
        jnp.einsum("gjqk,kgd->qgjd", dscores, key_heads, preferred_element_type=jnp.float32) * scale
    ).astype(jnp.bfloat16)
    key_grad = jnp.einsum("gjqk,qgjd->kgd", dscores, q4, preferred_element_type=jnp.float32) * scale
    value_grad = jnp.einsum("gjqk,qgjd->kgd", probs_low, do4, preferred_element_type=jnp.float32)
    attended_flat = attended.astype(jnp.bfloat16).reshape(tok_rows, heads_local * head_size)
    q_grad_flat = q_grad.reshape(tok_rows, heads_local * head_size)
    grad_terms = jnp.stack([key_grad, value_grad], axis=2).reshape(seq_rows, 2 * kv_width)
    grad_parts = lax.all_to_all(
        grad_terms.astype(jnp.bfloat16), plane, split_axis=0, concat_axis=1, tiled=True
    )
    grad_parts = grad_parts.reshape(kv_rows, ctx_count, tp_count * kv_local, 2, head_size)
    own_grads = jnp.sum(grad_parts.astype(jnp.float32), axis=1)
    k_grad_tokens = own_grads[:, :, 0, :].reshape(kv_rows, -1)
    v_grad_tokens = own_grads[:, :, 1, :].reshape(kv_rows, -1)
    return (attended_flat[None], q_grad_flat[None], k_grad_tokens[None], v_grad_tokens[None])


def solution(mesh):
    in_specs = (
        P(),
        P(),
        P("section", None, "ctx", "tp"),
        P("section", None, ("ctx", "tp"), None),
        P("section", None, ("ctx", "tp"), None),
        P("section", "ctx", "tp"),
    )
    out_specs = (
        P("section", "ctx", "tp"),
        P("section", "ctx", "tp"),
        P("section", ("ctx", "tp"), None),
        P("section", ("ctx", "tp"), None),
    )
    return jax.shard_map(body, mesh=mesh, in_specs=in_specs, out_specs=out_specs, check_vma=False)
```

profile of v0, /device:TPU:1, one launch (start us, length us, event | category | flops | bytes accessed | tf_op | source)
XLA Modules:
  0.0 97.7 jit_solution(3275048713458376290)
XLA Ops:
  0.6 1.2 %dynamic_slice.8 = s32[1]{0:T(128)} dynamic-slice(s32[8]{0:T(128)} %param.7, s32[]{:T(128)S(6)} %select_n.63), dynamic_slice_sizes={1} | dynamic-slice | bytes 12 | tf_op jit(solution)/shard_map/jit(dynamic_index_in_dim)/dynamic_slice | solution.py:32
  2.5 1.6 %fusion.32 = (bf16[22,1024]{1,0:T(8,128)(2,1)S(1)}, bf16[22,1024]{1,0:T(8,128)(2,1)S(1)}) fusion(pred[]{:T(512)} %bitcast, bf16[1,2,22,1024]{3,1,2,0:T(2,128)(2,1)} %param.9, bf16[1,2,22,1024]{3,1,2,0:T(2,128)(2,1)} %param.10), kind=kLoop, calls=%fused_computation.40 | loop fusion | flops 45056 | bytes 270337 | tf_op jit(solution)/shard_map/jit(_where)/select_n | solution.py:38
  4.2 0.1 copy.55
  4.3 4.8 %collective-permute-start = (bf16[22,2048]{1,0:T(8,128)(2,1)S(1)}, bf16[22,2048]{1,0:T(8,128)(2,1)S(1)}, u32[]{:S(2)}, u32[]{:S(2)}) collective-permute-start(bf16[22,2048]{1,0:T(8,128)(2,1)S(1)} %reshape.224), channel_id=1, source_target_pairs={{448,0},{0,64},{64,128},{128,192},{192,256},{256,320},{320,384},{3... | collective-permute-start | bytes 270344 | tf_op jit(solution)/shard_map/ppermute | solution.py:13
  9.1 8.6 %collective-permute-start.2 = (bf16[176,1024]{1,0:T(8,128)(2,1)}, bf16[176,1024]{1,0:T(8,128)(2,1)S(1)}, u32[]{:S(2)}, u32[]{:S(2)}) collective-permute-start(bf16[176,1024]{1,0:T(8,128)(2,1)} %bitcast.165), channel_id=1, source_target_pairs={{64,0},{128,64},{192,128},{256,192},{320,256},{384,320},{448,384},... | collective-permute-start | bytes 1081352 | tf_op jit(solution)/shard_map/ppermute | solution.py:13
  17.7 0.6 collective-permute-done
  18.4 0.9 broadcast_in_dim.17
  19.3 11.4 %all-to-all-start = ((bf16[64,22,256]{2,1,0:T(8,128)(2,1)}), bf16[64,22,256]{2,1,0:T(8,128)(2,1)S(1)}, u32[]{:S(2)}, u32[]{:S(2)}) async-start(bf16[64,22,256]{2,1,0:T(8,128)(2,1)} %bitcast.3), calls=%async_computation | async-start | bytes 1572864 | tf_op jit(solution)/shard_map/all_to_all | solution.py:53
  30.7 1.1 %select_bitcast_fusion = bf16[176,1024]{1,0:T(8,128)(2,1)S(1)} fusion(bf16[1,2,176,1024]{3,2,1,0:T(8,128)(2,1)} %param.8, pred[]{:T(512)} %bitcast), kind=kLoop, calls=%fused_computation.35 | loop fusion | flops 180224 | bytes 1081345 | tf_op jit(solution)/shard_map/jit(_where)/select_n | solution.py:38
  31.8 1.9 %collective-permute-start.1 = (bf16[176,1024]{1,0:T(8,128)(2,1)S(1)}, bf16[176,1024]{1,0:T(8,128)(2,1)S(1)}, u32[]{:S(2)}, u32[]{:S(2)}) collective-permute-start(bf16[176,1024]{1,0:T(8,128)(2,1)S(1)} %select_bitcast_fusion), channel_id=1, source_target_pairs={{448,0},{0,64},{64,128},{128,192},{192,256},{256,320},{320,384},{3... | collective-permute-start | bytes 1081352 | tf_op jit(solution)/shard_map/ppermute | solution.py:13
  33.7 0.7 broadcast_multiply_fusion
  34.4 0.1 add.65
  34.5 0.1 iota_add_fusion
  34.6 0.1 add.64
  34.6 0.1 add.66
  34.7 0.1 add.67
  34.8 0.1 add.69
  34.9 0.2 broadcast_compare_fusion
  35.1 0.0 collective-permute-done.2
  35.1 0.1 convert_bitcast_fusion.1
  35.2 0.1 copy.78
  35.3 9.1 %collective-permute-done.1 = bf16[176,1024]{1,0:T(8,128)(2,1)S(1)} collective-permute-done((bf16[176,1024]{1,0:T(8,128)(2,1)S(1)}, bf16[176,1024]{1,0:T(8,128)(2,1)S(1)}, u32[]{:S(2)}, u32[]{:S(2)}) %collective-permute-start.1) | collective-permute-done | bytes 360480 | tf_op jit(solution)/shard_map/ppermute | solution.py:13
  44.4 0.8 copy.79
  45.2 9.2 %all-to-all-done = bf16[64,22,256]{2,1,0:T(8,128)(2,1)S(1)} async-done(((bf16[64,22,256]{2,1,0:T(8,128)(2,1)}), bf16[64,22,256]{2,1,0:T(8,128)(2,1)S(1)}, u32[]{:S(2)}, u32[]{:S(2)}) %all-to-all-start) | async-done | bytes 720928 | tf_op jit(solution)/shard_map/all_to_all | solution.py:53
  54.5 0.3 reshape.226
  54.8 1.1 %fusion.34 = (bf16[1408,1,1,128]{3,2,0,1:T(2,128)(2,1)S(1)}, bf16[1408,1,1,128]{3,2,0,1:T(2,128)(2,1)S(1)}) fusion(bf16[1408,1,2,128]{3,2,0,1:T(2,128)(2,1)S(1)} %reshape.226), kind=kLoop, calls=%fused_computation.50 | loop fusion | bytes 1441792 | tf_op jit(solution)/shard_map/slice | solution.py:56
  55.8 1.9 %fusion.36 = (f32[8,176]{1,0:T(8,128)S(1)}, f32[1,8,176,1408]{3,2,1,0:T(8,128)S(1)}) fusion(bf16[1408,1,1,128]{3,2,0,1:T(2,128)(2,1)S(1)} %get-tuple-element.11, pred[176,1408]{1,0:T(8,128)(4,1)S(1)} %broadcast_compare_fusion, bf16[176,1024]{1,0:T(8,128)(2,1)S(1)} %collective-permute-done.1), kind=kOutput, calls=%fused_computation.52 | convolution fusion | flops 513456768 | bytes 8904192 | tf_op jit(solution)/shard_map/qgjd,kgd->gjqk/dot_general | solution.py:66
  57.7 1.2 %exponential_reduce_fusion = f32[8,176]{1,0:T(8,128)S(1)} fusion(f32[1,8,176,1408]{3,2,1,0:T(8,128)S(1)} %get-tuple-element.15, f32[8,176]{1,0:T(8,128)S(1)} %get-tuple-element.14), kind=kLoop, calls=%fused_computation.5 | loop fusion | flops 3963520 | bytes 7941120 | tf_op jit(solution)/shard_map/reduce_sum | solution.py:69
  59.0 1.7 %fusion.25 = (f32[176,8]{0,1:T(8,128)S(1)}, bf16[176,1,8,128]{3,0,2,1:T(8,128)(2,1)S(1)}) fusion(f32[176,1,8,128]{3,2,0,1:T(8,128)S(1)} %bitcast.152, f32[1,8,176,1408]{3,2,1,0:T(8,128)S(1)} %get-tuple-element.15, f32[8,176]{1,0:T(8,128)S(1)} %log_add_fusion, bf16[1408,1,1,128]{3,2,0,1:T(2,128)(2,1)S(1)} %get-tuple-element.10), kind=kOutput, calls=%fused_computation.26 | convolution fusion | flops 512014976 | bytes 9382912 | tf_op jit(solution)/shard_map/gjqk,kgd->qgjd/dot_general | solution.py:73
  60.7 0.0 copy-start.1
  60.7 2.2 %fusion.6 = bf16[8,176,1408]{2,1,0:T(8,128)(2,1)S(1)} fusion(f32[8,176]{1,0:T(8,128)S(1)} %bitcast.163, f32[1,8,176,1408]{3,2,1,0:T(8,128)S(1)} %get-tuple-element.15, f32[8,176]{1,0:T(8,128)S(1)} %log_add_fusion, bf16[1408,1,1,128]{3,2,0,1:T(2,128)(2,1)S(1)} %get-tuple-element.10, bf16[176,1024]{1,0:T(8,128)(2,1)S(1)} %collective-permute-done.2), kind=kOutput, calls=%fused_computation.10 | convolution fusion | flops 515440640 | bytes 12626944 | tf_op jit(solution)/shard_map/qgjd,kgd->gjqk/dot_general | solution.py:77
  62.9 0.0 copy-start
  62.9 0.0 copy-done.1
  62.9 0.9 fusion.17
  63.8 1.5 %fusion.20 = bf16[1408,1,1,128]{0,3,2,1:T(8,128)(2,1)S(1)} fusion(f32[1,8,176,1408]{3,2,1,0:T(8,128)S(1)} %get-tuple-element.15, f32[8,176]{1,0:T(8,128)S(1)} %log_add_fusion, bf16[176,1024]{1,0:T(8,128)(2,1)S(1)} %collective-permute-done.2), kind=kOutput, calls=%fused_computation.17 | convolution fusion | flops 511655936 | bytes 8656384 | tf_op jit(solution)/shard_map/gjqk,qgjd->kgd/dot_general | solution.py:83
  65.3 0.0 copy-done
  65.3 0.1 pad_maximum_fusion
  65.4 1.0 %copy.67 = bf16[1408,1,2,128]{3,2,0,1:T(2,128)(2,1)S(1)} copy(bf16[1408,1,2,128]{0,3,2,1:T(8,128)(2,1)S(1)} %pad_maximum_fusion) | data formatting | bytes 1441792 | tf_op jit(solution)/shard_map/stack | solution.py:86
  66.5 1.3 %convert_element_type.54 = bf16[64,22,256]{2,1,0:T(8,128)(2,1)} reshape(bf16[1408,1,2,128]{3,2,0,1:T(2,128)(2,1)S(1)} %copy.67) | data formatting | bytes 1441792 | tf_op jit(solution)/shard_map/convert_element_type | solution.py:88
  67.8 4.9 %all-to-all-start.1 = ((bf16[64,22,256]{2,1,0:T(8,128)(2,1)}), bf16[64,22,256]{2,1,0:T(8,128)(2,1)S(1)}, u32[]{:S(2)}, u32[]{:S(2)}) async-start(bf16[64,22,256]{2,1,0:T(8,128)(2,1)} %convert_element_type.54), calls=%async_computation.1 | async-start | bytes 1572864 | tf_op jit(solution)/shard_map/all_to_all | solution.py:87
  72.7 0.1 copy.60
  72.8 0.9 broadcast_in_dim_reshape.6
  73.7 3.3 %fusion.22 = bf16[176,1,8,128]{3,0,2,1:T(8,128)(2,1)S(1)} fusion(bf16[8,176,1408]{2,1,0:T(8,128)(2,1)} %copy-done, bf16[1408,1,1,128]{3,2,0,1:T(2,128)(2,1)S(1)} %get-tuple-element.11), kind=kOutput, calls=%fused_computation.23 | convolution fusion | flops 507871232 | bytes 4685824 | tf_op jit(solution)/shard_map/gjqk,kgd->qgjd/dot_general | solution.py:80
  77.0 0.1 copy.63
  77.1 0.9 broadcast_in_dim_reshape.7
  78.0 18.5 %all-to-all-done.1 = bf16[64,22,256]{2,1,0:T(8,128)(2,1)S(1)} async-done(((bf16[64,22,256]{2,1,0:T(8,128)(2,1)}), bf16[64,22,256]{2,1,0:T(8,128)(2,1)S(1)}, u32[]{:S(2)}, u32[]{:S(2)}) %all-to-all-start.1) | async-done | bytes 720928 | tf_op jit(solution)/shard_map/all_to_all | solution.py:87
  96.5 0.1 convert_bitcast_fusion
  96.7 0.4 bitcast_reduce_fusion
  97.1 0.7 fusion.35
  (12 shorter events, 0.2 us)
Async XLA Ops:
  4.3 14.0 %collective-permute-start = (bf16[22,2048]{1,0:T(8,128)(2,1)S(1)}, bf16[22,2048]{1,0:T(8,128)(2,1)S(1)}, u32[]{:S(2)}, u32[]{:S(2)}) collective-permute-start(bf16[22,2048]{1,0:T(8,128)(2,1)S(1)} %reshape.224), channel_id=1, source_target_pairs={{448,0},{0,64},{64,128},{128,192},{192,256},{256,320},{320,384},{3... | collective-permute-start | bytes 270344 | tf_op jit(solution)/shard_map/ppermute | solution.py:13
  9.1 26.0 %collective-permute-start.2 = (bf16[176,1024]{1,0:T(8,128)(2,1)}, bf16[176,1024]{1,0:T(8,128)(2,1)S(1)}, u32[]{:S(2)}, u32[]{:S(2)}) collective-permute-start(bf16[176,1024]{1,0:T(8,128)(2,1)} %bitcast.165), channel_id=1, source_target_pairs={{64,0},{128,64},{192,128},{256,192},{320,256},{384,320},{448,384},... | collective-permute-start | bytes 1081352 | tf_op jit(solution)/shard_map/ppermute | solution.py:13
  19.3 35.2 %all-to-all-start = ((bf16[64,22,256]{2,1,0:T(8,128)(2,1)}), bf16[64,22,256]{2,1,0:T(8,128)(2,1)S(1)}, u32[]{:S(2)}, u32[]{:S(2)}) async-start(bf16[64,22,256]{2,1,0:T(8,128)(2,1)} %bitcast.3), calls=%async_computation | async-start | bytes 1572864 | tf_op jit(solution)/shard_map/all_to_all | solution.py:53
  31.8 12.6 %collective-permute-start.1 = (bf16[176,1024]{1,0:T(8,128)(2,1)S(1)}, bf16[176,1024]{1,0:T(8,128)(2,1)S(1)}, u32[]{:S(2)}, u32[]{:S(2)}) collective-permute-start(bf16[176,1024]{1,0:T(8,128)(2,1)S(1)} %select_bitcast_fusion), channel_id=1, source_target_pairs={{448,0},{0,64},{64,128},{128,192},{192,256},{256,320},{320,384},{3... | collective-permute-start | bytes 1081352 | tf_op jit(solution)/shard_map/ppermute | solution.py:13
  60.7 2.2 %copy-start.1 = (bf16[22,8,8,128]{3,2,1,0:T(8,128)(2,1)S(1)}, bf16[22,8,8,128]{3,2,1,0:T(8,128)(2,1)}, u32[]{:S(2)}) copy-start(bf16[22,8,8,128]{3,2,1,0:T(8,128)(2,1)} %copy.79) | copy-start | bytes 1081348
  62.9 2.4 %copy-start = (bf16[8,176,1408]{2,1,0:T(8,128)(2,1)}, bf16[8,176,1408]{2,1,0:T(8,128)(2,1)S(1)}, u32[]{:S(2)}) copy-start(bf16[8,176,1408]{2,1,0:T(8,128)(2,1)S(1)} %fusion.6) | copy-start | bytes 11894788
  67.8 28.7 %all-to-all-start.1 = ((bf16[64,22,256]{2,1,0:T(8,128)(2,1)}), bf16[64,22,256]{2,1,0:T(8,128)(2,1)S(1)}, u32[]{:S(2)}, u32[]{:S(2)}) async-start(bf16[64,22,256]{2,1,0:T(8,128)(2,1)} %convert_element_type.54), calls=%async_computation.1 | async-start | bytes 1572864 | tf_op jit(solution)/shard_map/all_to_all | solution.py:87
where the time goes:
time: 98.2 us; the launch traced here: 97.7 us
  waiting for transfers between devices  37.4 us (38%)
  starting transfers between devices  31.6 us (32%)
  matrix products  11.5 us (12%)
  local copies, waits for them, and re-layouts  10.1 us (10%)
  other arithmetic  5.55 us (6%)
  between operations  1.6 us (2%)
    all_to_all x1, waiting for transfers between devices, body(): lax.all_to_all(grad_terms.astype(jnp.bfloat16), plane, split_axis=0, conc...  18.5 us
    ppermute x3, starting transfers between devices, passed_along(): return lax.ppermute(block, axis, route)  15.3 us
    all_to_all x1, starting transfers between devices, body(): lax.all_to_all(kv_pieces, plane, split_axis=0, concat_axis=0, tiled=True)  11.4 us
    ppermute x3, waiting for transfers between devices, passed_along(): return lax.ppermute(block, axis, route)  9.64 us
    all_to_all x1, waiting for transfers between devices, body(): lax.all_to_all(kv_pieces, plane, split_axis=0, concat_axis=0, tiled=True)  9.24 us
    all_to_all x1, starting transfers between devices, body(): lax.all_to_all(grad_terms.astype(jnp.bfloat16), plane, split_axis=0, conc...  4.92 us
    dot_general x1, matrix products, body(): jnp.einsum('gjqk,kgd->qgjd', dscores, key_heads, preferred_element_type=j...  3.31 us
    select_n x2, other arithmetic, pick(): chosen = jnp.where(wanted == slot, slots[slot], chosen)  2.7 us
  transfers between devices with their start and end apart: 5, of which 4 were waited for; matrix products, arithmetic and copies ran while one was open for 10% of the time, Pallas kernels for 0%

commit v1 on v0

--- a/solution.py
+++ b/solution.py
@@ -84,9 +84,15 @@
     attended_flat = attended.astype(jnp.bfloat16).reshape(tok_rows, heads_local * head_size)
     q_grad_flat = q_grad.reshape(tok_rows, heads_local * head_size)
     grad_terms = jnp.stack([key_grad, value_grad], axis=2).reshape(seq_rows, 2 * kv_width)
-    grad_parts = lax.all_to_all(
-        grad_terms.astype(jnp.bfloat16), plane, split_axis=0, concat_axis=1, tiled=True
-    )
+
+    def match_inputs_for(t0):
+        parts_out = jnp.concatenate(
+            lax.all_to_all(jnp.stack(jnp.split(t0, lax.axis_size(plane), 0), axis=0), plane, 0, 0),
+            1,
+        )
+        return parts_out
+
+    grad_parts = match_inputs_for(grad_terms.astype(jnp.bfloat16))
     grad_parts = grad_parts.reshape(kv_rows, ctx_count, tp_count * kv_local, 2, head_size)
     own_grads = jnp.sum(grad_parts.astype(jnp.float32), axis=1)
     k_grad_tokens = own_grads[:, :, 0, :].reshape(kv_rows, -1)

time: 98.2 us -> 205 us (2.09); the launches traced: 97.7 us -> 202 us
  local copies, waits for them, and re-layouts: 10.1 us -> 110 us
  other arithmetic: 5.55 us -> 9.72 us
    unnamed x9 -> x76, local copies, waits for them, and re-layouts: 0.99 us -> 59.2 us
    another operation x1 -> x65, local copies, waits for them, and re-layouts: 1.04 us -> 45.1 us  [match_inputs_for(): jnp.stack(jnp.split(t0, lax.axis_size(plane), 0), axis=0)]
    another operation x1 -> x8, other arithmetic: 0.08 us -> 4.66 us  [body(): jnp.stack([key_grad, value_grad], axis=2).reshape(seq_rows, 2 * kv_width)]
  transfers between devices with their start and end apart: 5 -> 5, of which waited for: 4 -> 4; matrix products, arithmetic and copies ran while one was open for 10% -> 5% of each run, Pallas kernels for 0% -> 0%
where the time goes in v1:
time: 205 us; the launch traced here: 202 us
  local copies, waits for them, and re-layouts  110 us (54%)
  waiting for transfers between devices  37.4 us (18%)
  starting transfers between devices  31.6 us (15%)
  matrix products  11.7 us (6%)
  other arithmetic  9.72 us (5%)
    unnamed x76, local copies, waits for them, and re-layouts  59.2 us
    another operation x65, local copies, waits for them, and re-layouts, match_inputs_for(): jnp.stack(jnp.split(t0, lax.axis_size(plane), 0), axis=0)  45.1 us
    all_to_all x1, waiting for transfers between devices, match_inputs_for(): lax.all_to_all(jnp.stack(jnp.split(t0, lax.axis_size(plane), 0), axis=0),...  18.5 us
    ppermute x3, starting transfers between devices, passed_along(): return lax.ppermute(block, axis, route)  15.3 us
    all_to_all x1, starting transfers between devices, body(): lax.all_to_all(kv_pieces, plane, split_axis=0, concat_axis=0, tiled=True)  11.4 us
    ppermute x3, waiting for transfers between devices, passed_along(): return lax.ppermute(block, axis, route)  9.64 us
    all_to_all x1, waiting for transfers between devices, body(): lax.all_to_all(kv_pieces, plane, split_axis=0, concat_axis=0, tiled=True)  9.24 us
    all_to_all x1, starting transfers between devices, match_inputs_for(): lax.all_to_all(jnp.stack(jnp.split(t0, lax.axis_size(plane), 0), axis=0),...  4.93 us
  transfers between devices with their start and end apart: 5, of which 4 were waited for; matrix products, arithmetic and copies ran while one was open for 5% of the time, Pallas kernels for 0%

profile of v1, /device:TPU:1, one launch (start us, length us, event | category | flops | bytes accessed | tf_op | source)
XLA Modules:
  0.0 202.5 jit_solution(9806546365954500626)
XLA Ops:
  2.5 1.6 fusion.32
  4.3 4.8 %collective-permute-start = (bf16[22,2048]{1,0:T(8,128)(2,1)S(1)}, bf16[22,2048]{1,0:T(8,128)(2,1)S(1)}, u32[]{:S(2)}, u32[]{:S(2)}) collective-permute-start(bf16[22,2048]{1,0:T(8,128)(2,1)S(1)} %reshape.347), channel_id=1, source_target_pairs={{448,0},{0,64},{64,128},{128,192},{192,256},{256,320},{320,384},{3... | collective-permute-start | bytes 270344 | tf_op jit(solution)/shard_map/ppermute | solution.py:13
  9.1 8.6 %collective-permute-start.2 = (bf16[176,1024]{1,0:T(8,128)(2,1)}, bf16[176,1024]{1,0:T(8,128)(2,1)S(1)}, u32[]{:S(2)}, u32[]{:S(2)}) collective-permute-start(bf16[176,1024]{1,0:T(8,128)(2,1)} %bitcast.291), channel_id=1, source_target_pairs={{64,0},{128,64},{192,128},{256,192},{320,256},{384,320},{448,384},... | collective-permute-start | bytes 1081352 | tf_op jit(solution)/shard_map/ppermute | solution.py:13
  19.3 11.4 %all-to-all-start = ((bf16[64,22,256]{2,1,0:T(8,128)(2,1)}), bf16[64,22,256]{2,1,0:T(8,128)(2,1)S(1)}, u32[]{:S(2)}, u32[]{:S(2)}) async-start(bf16[64,22,256]{2,1,0:T(8,128)(2,1)} %bitcast.3), calls=%async_computation | async-start | bytes 1572864 | tf_op jit(solution)/shard_map/all_to_all | solution.py:53
  31.8 1.9 collective-permute-start.1
  35.4 9.1 %collective-permute-done.1 = bf16[176,1024]{1,0:T(8,128)(2,1)S(1)} collective-permute-done((bf16[176,1024]{1,0:T(8,128)(2,1)S(1)}, bf16[176,1024]{1,0:T(8,128)(2,1)S(1)}, u32[]{:S(2)}, u32[]{:S(2)}) %collective-permute-start.1) | collective-permute-done | bytes 360480 | tf_op jit(solution)/shard_map/ppermute | solution.py:13
  45.2 9.2 %all-to-all-done = bf16[64,22,256]{2,1,0:T(8,128)(2,1)S(1)} async-done(((bf16[64,22,256]{2,1,0:T(8,128)(2,1)}), bf16[64,22,256]{2,1,0:T(8,128)(2,1)S(1)}, u32[]{:S(2)}, u32[]{:S(2)}) %all-to-all-start) | async-done | bytes 720928 | tf_op jit(solution)/shard_map/all_to_all | solution.py:53
  55.8 1.9 fusion.99
  59.0 1.7 fusion.25
  60.7 2.4 %fusion.6 = bf16[8,176,1408]{2,1,0:T(8,128)(2,1)S(1)} fusion(f32[8,176]{1,0:T(8,128)S(1)} %bitcast.289, f32[1,8,176,1408]{3,2,1,0:T(8,128)S(1)} %get-tuple-element.86, f32[8,176]{1,0:T(8,128)S(1)} %log_add_fusion, bf16[1408,1,1,128]{3,2,0,1:T(2,128)(2,1)S(1)} %get-tuple-element.81, bf16[176,1024]{1,0:T(8,128)(2,1)S(1)} %collective-permute-done.2), kind=kOutput, calls=%fused_computation.136 | convolution fusion | flops 515440640 | bytes 12626944 | tf_op jit(solution)/shard_map/qgjd,kgd->gjqk/dot_general | solution.py:77
  64.0 1.5 fusion.20
  71.8 1.5 copy.198
  73.3 1.5 copy.199
  74.8 1.5 copy.200
  76.4 1.5 copy.201
  77.9 1.5 copy.202
  79.4 1.5 copy.203
  81.0 1.5 copy.204
  82.5 1.5 copy.205
  84.0 1.5 copy.206
  85.5 1.5 copy.207
  87.1 1.5 copy.208
  88.6 1.5 copy.209
  90.1 1.5 copy.210
  91.7 1.5 copy.211
  93.2 1.5 copy.212
  94.7 1.5 copy.213
  96.2 1.5 copy.214
  97.8 1.5 copy.215
  99.3 1.5 copy.216
  100.8 1.5 copy.217
  102.4 1.5 copy.218
  103.9 1.5 copy.219
  105.4 1.5 copy.220
  107.0 1.5 copy.221
  108.5 1.5 copy.222
  110.0 1.5 copy.223
  115.4 1.3 constant_dynamic-update-slice_fusion.62
  116.7 1.3 constant_dynamic-update-slice_fusion.61
  118.0 1.3 constant_dynamic-update-slice_fusion.60
  119.3 1.3 constant_dynamic-update-slice_fusion.59
  120.6 1.3 constant_dynamic-update-slice_fusion.58
  121.9 1.3 constant_dynamic-update-slice_fusion.57
  123.2 1.3 constant_dynamic-update-slice_fusion.56
  124.5 1.3 constant_dynamic-update-slice_fusion.55
  127.1 1.3 constant_dynamic-update-slice_fusion.53
  128.4 1.3 constant_dynamic-update-slice_fusion.52
  129.7 1.3 constant_dynamic-update-slice_fusion.51
  131.0 1.3 constant_dynamic-update-slice_fusion.50
  132.4 1.3 constant_dynamic-update-slice_fusion.49
  133.7 1.3 constant_dynamic-update-slice_fusion.48
  135.0 1.3 constant_dynamic-update-slice_fusion.47
  136.3 1.3 constant_dynamic-update-slice_fusion.46
  137.6 1.3 constant_dynamic-update-slice_fusion.45
  138.9 1.3 constant_dynamic-update-slice_fusion.44
  140.2 1.3 constant_dynamic-update-slice_fusion.43
  141.5 1.3 constant_dynamic-update-slice_fusion.42
  142.8 1.3 constant_dynamic-update-slice_fusion.41
  145.4 1.3 constant_dynamic-update-slice_fusion.39
  146.7 1.3 constant_dynamic-update-slice_fusion.38
  148.0 1.3 constant_dynamic-update-slice_fusion.37
  171.5 4.9 %all-to-all-start.1 = ((bf16[64,22,256]{2,1,0:T(8,128)(2,1)}), bf16[64,22,256]{2,1,0:T(8,128)(2,1)S(1)}, u32[]{:S(2)}, u32[]{:S(2)}) async-start(bf16[64,22,256]{2,1,0:T(8,128)(2,1)} %constant_dynamic-update-slice_fusion), calls=%async_computation.1 | async-start | bytes 1572864 | tf_op jit(solution)/shard_map/all_to_all | solution.py:90
  177.4 3.3 %fusion.22 = bf16[176,1,8,128]{3,0,2,1:T(8,128)(2,1)S(1)} fusion(bf16[8,176,1408]{2,1,0:T(8,128)(2,1)} %copy-done, bf16[1408,1,1,128]{3,2,0,1:T(2,128)(2,1)S(1)} %get-tuple-element.82), kind=kOutput, calls=%fused_computation.148 | convolution fusion | flops 507871232 | bytes 4685824 | tf_op jit(solution)/shard_map/gjqk,kgd->qgjd/dot_general | solution.py:80
  181.7 18.5 %all-to-all-done.1 = bf16[64,22,256]{2,1,0:T(8,128)(2,1)S(1)} async-done(((bf16[64,22,256]{2,1,0:T(8,128)(2,1)}), bf16[64,22,256]{2,1,0:T(8,128)(2,1)S(1)}, u32[]{:S(2)}, u32[]{:S(2)}) %all-to-all-start.1) | async-done | bytes 720928 | tf_op jit(solution)/shard_map/all_to_all | solution.py:90
  (133 shorter events, 48.8 us)
Async XLA Ops:
  4.3 14.0 %collective-permute-start = (bf16[22,2048]{1,0:T(8,128)(2,1)S(1)}, bf16[22,2048]{1,0:T(8,128)(2,1)S(1)}, u32[]{:S(2)}, u32[]{:S(2)}) collective-permute-start(bf16[22,2048]{1,0:T(8,128)(2,1)S(1)} %reshape.347), channel_id=1, source_target_pairs={{448,0},{0,64},{64,128},{128,192},{192,256},{256,320},{320,384},{3... | collective-permute-start | bytes 270344 | tf_op jit(solution)/shard_map/ppermute | solution.py:13
  9.1 26.0 %collective-permute-start.2 = (bf16[176,1024]{1,0:T(8,128)(2,1)}, bf16[176,1024]{1,0:T(8,128)(2,1)S(1)}, u32[]{:S(2)}, u32[]{:S(2)}) collective-permute-start(bf16[176,1024]{1,0:T(8,128)(2,1)} %bitcast.291), channel_id=1, source_target_pairs={{64,0},{128,64},{192,128},{256,192},{320,256},{384,320},{448,384},... | collective-permute-start | bytes 1081352 | tf_op jit(solution)/shard_map/ppermute | solution.py:13
  19.3 35.2 %all-to-all-start = ((bf16[64,22,256]{2,1,0:T(8,128)(2,1)}), bf16[64,22,256]{2,1,0:T(8,128)(2,1)S(1)}, u32[]{:S(2)}, u32[]{:S(2)}) async-start(bf16[64,22,256]{2,1,0:T(8,128)(2,1)} %bitcast.3), calls=%async_computation | async-start | bytes 1572864 | tf_op jit(solution)/shard_map/all_to_all | solution.py:53
  31.8 12.6 %collective-permute-start.1 = (bf16[176,1024]{1,0:T(8,128)(2,1)S(1)}, bf16[176,1024]{1,0:T(8,128)(2,1)S(1)}, u32[]{:S(2)}, u32[]{:S(2)}) collective-permute-start(bf16[176,1024]{1,0:T(8,128)(2,1)S(1)} %select_bitcast_fusion), channel_id=1, source_target_pairs={{448,0},{0,64},{64,128},{128,192},{192,256},{256,320},{320,384},{3... | collective-permute-start | bytes 1081352 | tf_op jit(solution)/shard_map/ppermute | solution.py:13
  60.7 2.4 %copy-start.1 = (bf16[22,8,8,128]{3,2,1,0:T(8,128)(2,1)S(1)}, bf16[22,8,8,128]{3,2,1,0:T(8,128)(2,1)}, u32[]{:S(2)}) copy-start(bf16[22,8,8,128]{3,2,1,0:T(8,128)(2,1)} %copy.278) | copy-start | bytes 1081348
  63.1 2.4 %copy-start = (bf16[8,176,1408]{2,1,0:T(8,128)(2,1)}, bf16[8,176,1408]{2,1,0:T(8,128)(2,1)S(1)}, u32[]{:S(2)}) copy-start(bf16[8,176,1408]{2,1,0:T(8,128)(2,1)S(1)} %fusion.6) | copy-start | bytes 11894788
  171.5 28.7 %all-to-all-start.1 = ((bf16[64,22,256]{2,1,0:T(8,128)(2,1)}), bf16[64,22,256]{2,1,0:T(8,128)(2,1)S(1)}, u32[]{:S(2)}, u32[]{:S(2)}) async-start(bf16[64,22,256]{2,1,0:T(8,128)(2,1)} %constant_dynamic-update-slice_fusion), calls=%async_computation.1 | async-start | bytes 1572864 | tf_op jit(solution)/shard_map/all_to_all | solution.py:90
